TPU v7x, 256 devices: a whole 4x4x8 slice. The times are simulated.
256 devices in a mesh: pos: 16 (over x_hi, z), exp: 16 (over y, x_lo, core).
Axes of the slice: x: 4 (x_hi: 2, x_lo: 2; x = x_hi * 2 + x_lo), y: 4, z: 8, core: 2. Of those that a mesh axis runs over, the one named last changes fastest.
Arguments:
- patches: bfloat16 [65536, 4, 256], P(('pos', 'exp')), may hold values from -6 to 6
- conv_weight: bfloat16 [3, 256, 2048], replicated, may hold values from -0.21875 to 0.21875
- phi: bfloat16 [2048, 128], replicated, may hold values from -40 to 40, as said below
- w_in: bfloat16 [16, 2048, 8192], P('exp', None, 'pos'), may hold values from -0.125 to 0.125
- w_out: bfloat16 [16, 8192, 2048], P('exp', 'pos'), may hold values from -0.0625 to 0.0625
Outputs:
- mixed: bfloat16 [65536, 4, 2048], P(('pos', 'exp'))
Inputs may be any that keep to these rules, and one draw needn't show every extreme that they name: phi is real-valued.
All inputs are finite; a program needn't handle non-finite values.
Results may differ from a plain program's by a relative error of at most 0.019.
The roundings to bfloat16 on the way count: a program that leaves them out, or rounds other values in their place, can miss the bound.
Values may be sent and summed in bfloat16 or wider, within the bound.
No kernel may reach another device: no remote copies, remote signals or barrier semaphores. Data moves between devices by JAX's collectives and lax.ppermute only.
A program may use at most 128 MiB of HBM per device.

v0:
```python
import jax
import jax.numpy as jnp
from jax import lax
from jax.sharding import PartitionSpec as P

D = 2048
SLOTS_PER = 8


def with_halo(array, sides, width):
    for axis, dim in sides:
        count, length = (lax.axis_size(axis), array.shape[dim])
        up = [(i, (i + 1) % count) for i in range(count - 1)]
        down = [(j, i) for i, j in up]
        last = lax.slice_in_dim(array, length - width, length, axis=dim)
        initial = lax.slice_in_dim(array, 0, width, axis=dim)
        before = lax.ppermute(last, axis, up)
        after = lax.ppermute(initial, axis, down)
        array = jnp.concatenate([before, array, after], axis=dim)
    return array


def butterfly_sum(value, axis):
    count = lax.axis_size(axis)
    step = 1
    while step < count:
        pairs = [(i, i ^ step) for i in range(count)]
        value = value + lax.ppermute(value, axis, pairs)
        step *= 2
    return value


def merge(mine, theirs):
    peak = jnp.maximum(mine[:, D], theirs[:, D])
    a = jnp.exp(mine[:, D] - peak)[:, None]
    b = jnp.exp(theirs[:, D] - peak)[:, None]
    merged = mine * a + theirs * b
    return merged.at[:, D].set(peak)


def butterfly_softmax_sum(value, axis):
    count = lax.axis_size(axis)
    step = 1
    while step < count:
        pairs = [(i, i ^ step) for i in range(count)]
        value = merge(value, lax.ppermute(value, axis, pairs))
        step *= 2
    return value


def per_device(patches, conv_weight, phi, w_in, w_out):
    channels, periods, samples = patches.shape
    every = ("pos", "exp")
    padded = with_halo(jnp.swapaxes(patches, 0, 1), ((every, 1),), 1)
    window = jnp.concatenate([padded[:, offset : offset + channels] for offset in range(3)], axis=2)
    window = window.reshape(periods * channels, 3 * samples)
    taps = conv_weight.reshape(3 * samples, D)
    flat = jnp.dot(window, taps, preferred_element_type=jnp.float32).astype(jnp.bfloat16)
    logits = jnp.dot(flat, phi, preferred_element_type=jnp.float32)
    slots = logits.shape[1]
    local_peak = jnp.max(logits, axis=0)
    raw_weights = jnp.exp(logits - local_peak)
    local_total = jnp.sum(raw_weights, axis=0)
    every_slot = lax.dot_general(
        raw_weights.astype(jnp.bfloat16),
        flat,
        (((0,), (0,)), ((), ())),
        preferred_element_type=jnp.float32,
    )
    extra = jnp.zeros((slots, 128), jnp.float32)
    extra = extra.at[:, 0].set(local_peak).at[:, 1].set(local_total)
    packed = jnp.concatenate([every_slot, extra], axis=1)
    groups = lax.axis_size("exp")
    mine = lax.all_to_all(packed, "exp", 0, 0, tiled=True).reshape(groups, SLOTS_PER, -1)
    peaks = mine[:, :, D]
    peak = jnp.max(peaks, axis=0)
    scale = jnp.exp(peaks - peak)
    sums = jnp.sum(mine[:, :, :D] * scale[:, :, None], axis=0)
    total = jnp.sum(mine[:, :, D + 1] * scale, axis=0)
    owned = jnp.concatenate(
        [sums, jnp.zeros((SLOTS_PER, 128), jnp.float32).at[:, 0].set(peak).at[:, 1].set(total)],
        axis=1,
    )
    owned = butterfly_softmax_sum(owned, "pos")
    slot_in = (owned[:, :D] / owned[:, D + 1 : D + 2]).astype(jnp.bfloat16)
    hidden = jax.nn.gelu(
        jnp.dot(slot_in, w_in[0], preferred_element_type=jnp.float32), approximate=True
    ).astype(jnp.bfloat16)
    expert_term = jnp.dot(hidden, w_out[0], preferred_element_type=jnp.float32)
    slot_out = butterfly_sum(expert_term, "pos").astype(jnp.bfloat16)
    row_peak = jnp.max(logits, axis=1, keepdims=True)
    row_weights = jnp.exp(logits - row_peak)
    combine = (row_weights / jnp.sum(row_weights, axis=1, keepdims=True)).astype(jnp.bfloat16)
    mixed = jnp.dot(
        combine,
        lax.all_gather(slot_out, "exp", axis=0, tiled=True),
        preferred_element_type=jnp.float32,
    )
    return jnp.swapaxes(mixed.astype(jnp.bfloat16).reshape(periods, channels, D), 0, 1)


def solution(mesh):
    in_specs = (
        P(("pos", "exp"), None, None),
        P(),
        P(),
        P("exp", None, "pos"),
        P("exp", "pos", None),
    )
    out_specs = P(("pos", "exp"), None, None)
    return jax.shard_map(
        per_device, mesh=mesh, in_specs=in_specs, out_specs=out_specs, check_vma=False
    )
```

profile of v0, /device:TPU:1, one launch (start us, length us, event | category | flops | bytes accessed | tf_op | source)
XLA Modules:
  0.0 136.0 jit_solution(183512765969925446)
XLA Ops:
  1.3 4.5 %collective-permute-start = (bf16[4,1,256]{2,1,0:T(2,128)(2,1)S(1)}, bf16[4,1,256]{2,1,0:T(2,128)(2,1)S(1)}, u32[]{:S(2)}, u32[]{:S(2)}) collective-permute-start(bf16[4,1,256]{2,1,0:T(2,128)(2,1)S(1)} %get-tuple-element.116), channel_id=1, source_target_pairs={{0,1},{1,2},{2,3},{3,4},{4,5},{5,6},{6,7},{7,8},{8,9},{9,10},{10,1... | collective-permute-start | bytes 6152 | tf_op jit(solution)/shard_map/ppermute | solution.py:17
  5.8 1.9 %collective-permute-start.1 = (bf16[4,1,256]{2,1,0:T(2,128)(2,1)S(1)}, bf16[4,1,256]{2,1,0:T(2,128)(2,1)S(1)}, u32[]{:S(2)}, u32[]{:S(2)}) collective-permute-start(bf16[4,1,256]{2,1,0:T(2,128)(2,1)S(1)} %get-tuple-element.117), channel_id=1, source_target_pairs={{1,0},{2,1},{3,2},{4,3},{5,4},{6,5},{7,6},{8,7},{9,8},{10,9},{11,1... | collective-permute-start | bytes 6152 | tf_op jit(solution)/shard_map/ppermute | solution.py:18
  9.1 1.6 %collective-permute-done.1 = bf16[4,1,256]{2,1,0:T(2,128)(2,1)S(1)} collective-permute-done((bf16[4,1,256]{2,1,0:T(2,128)(2,1)S(1)}, bf16[4,1,256]{2,1,0:T(2,128)(2,1)S(1)}, u32[]{:S(2)}, u32[]{:S(2)}) %collective-permute-start.1) | collective-permute-done | bytes 2080 | tf_op jit(solution)/shard_map/ppermute | solution.py:18
  11.0 3.6 %convolution_convert_fusion.1 = bf16[1024,2048]{1,0:T(8,128)(2,1)S(1)} fusion(bf16[1024,768]{1,0:T(8,128)(2,1)S(1)} %bitcast.53, bf16[768,2048]{1,0:T(8,128)(2,1)S(1)} %bitcast.49), kind=kOutput, calls=%fused_computation.2 | convolution fusion | flops 3223322624 | bytes 8912896 | tf_op jit(solution)/shard_map/dot_general | solution.py:58
  16.0 1.7 %fusion.10 = f32[128,2048]{1,0:T(8,128)} fusion(bf16[1024,2048]{1,0:T(8,128)(2,1)S(1)} %convolution_convert_fusion.1, f32[1024,128]{1,0:T(8,128)S(1)} %get-tuple-element.118, f32[128]{0:T(128)S(1)} %get-tuple-element.104), kind=kOutput, calls=%fused_computation.21 | convolution fusion | flops 537133056 | bytes 5767680 | tf_op jit(solution)/shard_map/dot_general | solution.py:64
  21.3 25.0 %all_to_all.9 = f32[16,8,2176]{2,1,0:T(8,128)S(1)} all-to-all(f32[16,8,2176]{2,1,0:T(8,128)S(1)} %maximum_bitcast_fusion), channel_id=1, replica_groups=mesh['pos'=16,'exp'=16] {'exp'}, dimensions={0} | all-to-all | bytes 2228224 | tf_op jit(solution)/shard_map/all_to_all | solution.py:74
  51.0 1.7 %collective-permute-start.2 = (f32[8,2176]{1,0:T(8,128)S(1)}, f32[8,2176]{1,0:T(8,128)S(1)}, u32[]{:S(2)}, u32[]{:S(2)}) collective-permute-start(f32[8,2176]{1,0:T(8,128)S(1)} %pad_maximum_fusion.2), channel_id=1, source_target_pairs={{0,16},{16,0},{32,48},{48,32},{64,80},{80,64},{96,112},{112,96},{1... | collective-permute-start | bytes 208904 | tf_op jit(solution)/shard_map/ppermute | solution.py:46
  55.7 5.6 %collective-permute-start.3 = (f32[8,2176]{1,0:T(8,128)S(1)}, f32[8,2176]{1,0:T(8,128)S(1)}, u32[]{:S(2)}, u32[]{:S(2)}) collective-permute-start(f32[8,2176]{1,0:T(8,128)S(1)} %scatter.30), channel_id=1, source_target_pairs={{0,32},{16,48},{32,0},{48,16},{64,96},{80,112},{96,64},{112,80},{1... | collective-permute-start | bytes 208904 | tf_op jit(solution)/shard_map/ppermute | solution.py:46
  61.3 1.7 %collective-permute-done.3 = f32[8,2176]{1,0:T(8,128)S(1)} collective-permute-done((f32[8,2176]{1,0:T(8,128)S(1)}, f32[8,2176]{1,0:T(8,128)S(1)}, u32[]{:S(2)}, u32[]{:S(2)}) %collective-permute-start.3) | collective-permute-done | bytes 69664 | tf_op jit(solution)/shard_map/ppermute | solution.py:46
  64.0 3.2 %collective-permute-start.4 = (f32[8,2176]{1,0:T(8,128)S(1)}, f32[8,2176]{1,0:T(8,128)S(1)}, u32[]{:S(2)}, u32[]{:S(2)}) collective-permute-start(f32[8,2176]{1,0:T(8,128)S(1)} %scatter.31), channel_id=1, source_target_pairs={{0,64},{16,80},{32,96},{48,112},{64,0},{80,16},{96,32},{112,48},{1... | collective-permute-start | bytes 208904 | tf_op jit(solution)/shard_map/ppermute | solution.py:46
  67.2 4.0 %collective-permute-done.4 = f32[8,2176]{1,0:T(8,128)S(1)} collective-permute-done((f32[8,2176]{1,0:T(8,128)S(1)}, f32[8,2176]{1,0:T(8,128)S(1)}, u32[]{:S(2)}, u32[]{:S(2)}) %collective-permute-start.4) | collective-permute-done | bytes 69664 | tf_op jit(solution)/shard_map/ppermute | solution.py:46
  72.2 2.8 %collective-permute-start.5 = (f32[8,2176]{1,0:T(8,128)S(1)}, f32[8,2176]{1,0:T(8,128)S(1)}, u32[]{:S(2)}, u32[]{:S(2)}) collective-permute-start(f32[8,2176]{1,0:T(8,128)S(1)} %scatter.34), channel_id=1, source_target_pairs={{0,128},{16,144},{32,160},{48,176},{64,192},{80,208},{96,224},{112... | collective-permute-start | bytes 208904 | tf_op jit(solution)/shard_map/ppermute | solution.py:46
  75.0 1.9 %collective-permute-done.5 = f32[8,2176]{1,0:T(8,128)S(1)} collective-permute-done((f32[8,2176]{1,0:T(8,128)S(1)}, f32[8,2176]{1,0:T(8,128)S(1)}, u32[]{:S(2)}, u32[]{:S(2)}) %collective-permute-start.5) | collective-permute-done | bytes 69664 | tf_op jit(solution)/shard_map/ppermute | solution.py:46
  77.4 3.0 %fusion = f32[8,2048]{1,0:T(8,128)S(1)} fusion(bf16[1,512,2048]{2,1,0:T(8,128)(2,1)} %param.25, bf16[1,2048,512]{2,1,0:T(8,128)(2,1)} %param.24, f32[8,2176]{1,0:T(8,128)S(1)} %multiply_add_fusion, f32[8]{0:T(128)S(1)} %slice_reduce_fusion), kind=kOutput, calls=%fused_computation.3 | convolution fusion | flops 33624064 | bytes 4325888 | tf_op jit(solution)/shard_map/dot_general | solution.py:89
  81.7 1.8 %collective-permute-done.6 = f32[8,2048]{1,0:T(8,128)S(1)} collective-permute-done((f32[8,2048]{1,0:T(8,128)S(1)}, f32[8,2048]{1,0:T(8,128)S(1)}, u32[]{:S(2)}, u32[]{:S(2)}) %collective-permute-start.6) | collective-permute-done | bytes 65568 | tf_op jit(solution)/shard_map/ppermute | solution.py:28
  83.5 2.9 %collective-permute-start.7 = (f32[8,2048]{1,0:T(8,128)S(1)}, f32[8,2048]{1,0:T(8,128)S(1)}, u32[]{:S(2)}, u32[]{:S(2)}) collective-permute-start(f32[8,2048]{1,0:T(8,128)S(1)} %add.60), channel_id=1, source_target_pairs={{0,32},{16,48},{32,0},{48,16},{64,96},{80,112},{96,64},{112,80},{1... | collective-permute-start | bytes 196616 | tf_op jit(solution)/shard_map/ppermute | solution.py:28
  86.4 1.7 %collective-permute-done.7 = f32[8,2048]{1,0:T(8,128)S(1)} collective-permute-done((f32[8,2048]{1,0:T(8,128)S(1)}, f32[8,2048]{1,0:T(8,128)S(1)}, u32[]{:S(2)}, u32[]{:S(2)}) %collective-permute-start.7) | collective-permute-done | bytes 65568 | tf_op jit(solution)/shard_map/ppermute | solution.py:28
  88.1 3.2 %collective-permute-start.8 = (f32[8,2048]{1,0:T(8,128)S(1)}, f32[8,2048]{1,0:T(8,128)S(1)}, u32[]{:S(2)}, u32[]{:S(2)}) collective-permute-start(f32[8,2048]{1,0:T(8,128)S(1)} %add.61), channel_id=1, source_target_pairs={{0,64},{16,80},{32,96},{48,112},{64,0},{80,16},{96,32},{112,48},{1... | collective-permute-start | bytes 196616 | tf_op jit(solution)/shard_map/ppermute | solution.py:28
  91.3 4.3 %collective-permute-done.8 = f32[8,2048]{1,0:T(8,128)S(1)} collective-permute-done((f32[8,2048]{1,0:T(8,128)S(1)}, f32[8,2048]{1,0:T(8,128)S(1)}, u32[]{:S(2)}, u32[]{:S(2)}) %collective-permute-start.8) | collective-permute-done | bytes 65568 | tf_op jit(solution)/shard_map/ppermute | solution.py:28
  95.6 3.7 %collective-permute-start.9 = (f32[8,2048]{1,0:T(8,128)S(1)}, f32[8,2048]{1,0:T(8,128)S(1)}, u32[]{:S(2)}, u32[]{:S(2)}) collective-permute-start(f32[8,2048]{1,0:T(8,128)S(1)} %add.62), channel_id=1, source_target_pairs={{0,128},{16,144},{32,160},{48,176},{64,192},{80,208},{96,224},{112... | collective-permute-start | bytes 196616 | tf_op jit(solution)/shard_map/ppermute | solution.py:28
  99.4 1.7 %collective-permute-done.9 = f32[8,2048]{1,0:T(8,128)S(1)} collective-permute-done((f32[8,2048]{1,0:T(8,128)S(1)}, f32[8,2048]{1,0:T(8,128)S(1)}, u32[]{:S(2)}, u32[]{:S(2)}) %collective-permute-start.9) | collective-permute-done | bytes 65568 | tf_op jit(solution)/shard_map/ppermute | solution.py:28
  101.0 27.4 %all_gather.3 = bf16[128,2048]{1,0:T(8,128)(2,1)S(1)} all-gather(bf16[8,2048]{1,0:T(8,128)(2,1)S(1)} %add_convert_fusion), channel_id=1, replica_groups=mesh['pos'=16,'exp'=16] {'exp'}, dimensions={0}, use_global_device_ids=true | all-gather | bytes 557056 | tf_op jit(solution)/shard_map/all_gather | solution.py:96
  128.4 2.4 %convolution_convert_fusion = bf16[1024,2048]{1,0:T(8,128)(2,1)S(1)} fusion(bf16[128,2048]{1,0:T(8,128)(2,1)S(1)} %all_gather.3, f32[1024,128]{1,0:T(8,128)} %copy-done.2, f32[1024]{0:T(1024)S(1)} %get-tuple-element.101, f32[1024]{0:T(1024)S(1)} %get-tuple-element.103), kind=kOutput, calls=%fused_computation.1 | convolution fusion | flops 539361280 | bytes 5251072 | tf_op jit(solution)/shard_map/dot_general | solution.py:94
  130.8 5.3 %copy.63 = bf16[4,256,2048]{2,0,1:T(4,128)(2,1)} copy(bf16[4,256,2048]{2,1,0:T(8,128)(2,1)S(1)} %bitcast.50) | data formatting | bytes 8388608 | tf_op jit(solution)/shard_map/reshape | solution.py:99
  (59 shorter events, 19.0 us)
Async XLA Ops:
  0.0 11.0 %copy-start = (bf16[3,256,2048]{2,1,0:T(8,128)(2,1)S(1)}, bf16[3,256,2048]{2,1,0:T(8,128)(2,1)}, u32[]{:S(2)}) copy-start(bf16[3,256,2048]{2,1,0:T(8,128)(2,1)} %param.22) | copy-start | bytes 9437188
  1.3 7.8 %collective-permute-start = (bf16[4,1,256]{2,1,0:T(2,128)(2,1)S(1)}, bf16[4,1,256]{2,1,0:T(2,128)(2,1)S(1)}, u32[]{:S(2)}, u32[]{:S(2)}) collective-permute-start(bf16[4,1,256]{2,1,0:T(2,128)(2,1)S(1)} %get-tuple-element.116), channel_id=1, source_target_pairs={{0,1},{1,2},{2,3},{3,4},{4,5},{5,6},{6,7},{7,8},{8,9},{9,10},{10,1... | collective-permute-start | bytes 6152 | tf_op jit(solution)/shard_map/ppermute | solution.py:17
  5.8 4.9 %collective-permute-start.1 = (bf16[4,1,256]{2,1,0:T(2,128)(2,1)S(1)}, bf16[4,1,256]{2,1,0:T(2,128)(2,1)S(1)}, u32[]{:S(2)}, u32[]{:S(2)}) collective-permute-start(bf16[4,1,256]{2,1,0:T(2,128)(2,1)S(1)} %get-tuple-element.117), channel_id=1, source_target_pairs={{1,0},{2,1},{3,2},{4,3},{5,4},{6,5},{7,6},{8,7},{9,8},{10,9},{11,1... | collective-permute-start | bytes 6152 | tf_op jit(solution)/shard_map/ppermute | solution.py:18
  11.0 3.7 %copy-start.3 = (bf16[2048,128]{1,0:T(8,128)(2,1)S(1)}, bf16[2048,128]{1,0:T(8,128)(2,1)}, u32[]{:S(2)}) copy-start(bf16[2048,128]{1,0:T(8,128)(2,1)} %param.23) | copy-start | bytes 1572868
  16.0 2.8 %copy-start.2 = (f32[1024,128]{1,0:T(8,128)}, f32[1024,128]{1,0:T(8,128)S(1)}, u32[]{:S(2)}) copy-start(f32[1024,128]{1,0:T(8,128)S(1)} %get-tuple-element.118) | copy-start | bytes 1572868
  46.4 1.0 copy-start.1
  51.0 3.7 %collective-permute-start.2 = (f32[8,2176]{1,0:T(8,128)S(1)}, f32[8,2176]{1,0:T(8,128)S(1)}, u32[]{:S(2)}, u32[]{:S(2)}) collective-permute-start(f32[8,2176]{1,0:T(8,128)S(1)} %pad_maximum_fusion.2), channel_id=1, source_target_pairs={{0,16},{16,0},{32,48},{48,32},{64,80},{80,64},{96,112},{112,96},{1... | collective-permute-start | bytes 208904 | tf_op jit(solution)/shard_map/ppermute | solution.py:46
  55.7 7.3 %collective-permute-start.3 = (f32[8,2176]{1,0:T(8,128)S(1)}, f32[8,2176]{1,0:T(8,128)S(1)}, u32[]{:S(2)}, u32[]{:S(2)}) collective-permute-start(f32[8,2176]{1,0:T(8,128)S(1)} %scatter.30), channel_id=1, source_target_pairs={{0,32},{16,48},{32,0},{48,16},{64,96},{80,112},{96,64},{112,80},{1... | collective-permute-start | bytes 208904 | tf_op jit(solution)/shard_map/ppermute | solution.py:46
  64.0 7.2 %collective-permute-start.4 = (f32[8,2176]{1,0:T(8,128)S(1)}, f32[8,2176]{1,0:T(8,128)S(1)}, u32[]{:S(2)}, u32[]{:S(2)}) collective-permute-start(f32[8,2176]{1,0:T(8,128)S(1)} %scatter.31), channel_id=1, source_target_pairs={{0,64},{16,80},{32,96},{48,112},{64,0},{80,16},{96,32},{112,48},{1... | collective-permute-start | bytes 208904 | tf_op jit(solution)/shard_map/ppermute | solution.py:46
  72.2 4.8 %collective-permute-start.5 = (f32[8,2176]{1,0:T(8,128)S(1)}, f32[8,2176]{1,0:T(8,128)S(1)}, u32[]{:S(2)}, u32[]{:S(2)}) collective-permute-start(f32[8,2176]{1,0:T(8,128)S(1)} %scatter.34), channel_id=1, source_target_pairs={{0,128},{16,144},{32,160},{48,176},{64,192},{80,208},{96,224},{112... | collective-permute-start | bytes 208904 | tf_op jit(solution)/shard_map/ppermute | solution.py:46
  80.4 3.1 %collective-permute-start.6 = (f32[8,2048]{1,0:T(8,128)S(1)}, f32[8,2048]{1,0:T(8,128)S(1)}, u32[]{:S(2)}, u32[]{:S(2)}) collective-permute-start(f32[8,2048]{1,0:T(8,128)S(1)} %fusion), channel_id=1, source_target_pairs={{0,16},{16,0},{32,48},{48,32},{64,80},{80,64},{96,112},{112,96},{1... | collective-permute-start | bytes 196616 | tf_op jit(solution)/shard_map/ppermute | solution.py:28
  83.5 4.6 %collective-permute-start.7 = (f32[8,2048]{1,0:T(8,128)S(1)}, f32[8,2048]{1,0:T(8,128)S(1)}, u32[]{:S(2)}, u32[]{:S(2)}) collective-permute-start(f32[8,2048]{1,0:T(8,128)S(1)} %add.60), channel_id=1, source_target_pairs={{0,32},{16,48},{32,0},{48,16},{64,96},{80,112},{96,64},{112,80},{1... | collective-permute-start | bytes 196616 | tf_op jit(solution)/shard_map/ppermute | solution.py:28
  88.1 7.5 %collective-permute-start.8 = (f32[8,2048]{1,0:T(8,128)S(1)}, f32[8,2048]{1,0:T(8,128)S(1)}, u32[]{:S(2)}, u32[]{:S(2)}) collective-permute-start(f32[8,2048]{1,0:T(8,128)S(1)} %add.61), channel_id=1, source_target_pairs={{0,64},{16,80},{32,96},{48,112},{64,0},{80,16},{96,32},{112,48},{1... | collective-permute-start | bytes 196616 | tf_op jit(solution)/shard_map/ppermute | solution.py:28
  95.6 5.4 %collective-permute-start.9 = (f32[8,2048]{1,0:T(8,128)S(1)}, f32[8,2048]{1,0:T(8,128)S(1)}, u32[]{:S(2)}, u32[]{:S(2)}) collective-permute-start(f32[8,2048]{1,0:T(8,128)S(1)} %add.62), channel_id=1, source_target_pairs={{0,128},{16,144},{32,160},{48,176},{64,192},{80,208},{96,224},{112... | collective-permute-start | bytes 196616 | tf_op jit(solution)/shard_map/ppermute | solution.py:28
where the time goes:
time: 136 us
  blocking collectives  52.4 us (39%)
  starting transfers between devices  30.9 us (23%)
  waiting for transfers between devices  20.1 us (15%)
  matrix products  12.1 us (9%)
  other arithmetic  11.2 us (8%)
  local copies, waits for them, and re-layouts  9.09 us (7%)
    all_gather x1, blocking collectives, per_device(): lax.all_gather(slot_out, 'exp', axis=0, tiled=True)  27.4 us
    all_to_all x1, blocking collectives, per_device(): lax.all_to_all(packed, 'exp', 0, 0, tiled=True)  25 us
    ppermute x4, starting transfers between devices, butterfly_softmax_sum(): value = merge(value, lax.ppermute(value, axis, pairs))  13.4 us
    ppermute x4, starting transfers between devices, butterfly_sum(): value = value + lax.ppermute(value, axis, pairs)  11.1 us
    ppermute x4, waiting for transfers between devices, butterfly_sum(): value = value + lax.ppermute(value, axis, pairs)  9.47 us
    ppermute x4, waiting for transfers between devices, butterfly_softmax_sum(): value = merge(value, lax.ppermute(value, axis, pairs))  8.97 us
    reshape x1, local copies, waits for them, and re-layouts, per_device(): mixed.astype(jnp.bfloat16).reshape(periods, channels, D)  5.25 us
    another operation x7, other arithmetic  4.53 us
  transfers between devices with their start and end apart: 10, of which 9 were waited for; matrix products, arithmetic and copies ran while one was open for 1% of the time, Pallas kernels for 0%

commit v1 on v0

--- a/solution.py
+++ b/solution.py
@@ -93,7 +93,9 @@
     combine = (row_weights / jnp.sum(row_weights, axis=1, keepdims=True)).astype(jnp.bfloat16)
     mixed = jnp.dot(
         combine,
-        lax.all_gather(slot_out, "exp", axis=0, tiled=True),
+        jnp.concatenate(
+            lax.all_to_all(jnp.stack([slot_out] * lax.axis_size("exp")), "exp", 0, 0), axis=0
+        ),
         preferred_element_type=jnp.float32,
     )
     return jnp.swapaxes(mixed.astype(jnp.bfloat16).reshape(periods, channels, D), 0, 1)

time: 136 us -> 130 us (0.956)
  blocking collectives: 52.4 us -> 45.3 us
    all_gather x1 -> x0, blocking collectives: 27.4 us -> none  [per_device(): lax.all_gather(slot_out, 'exp', axis=0, tiled=True)]
    all_to_all x0 -> x1, blocking collectives: none -> 20.3 us  [per_device(): lax.all_to_all(jnp.stack([slot_out] * lax.axis_size('exp')), 'exp', 0, 0)]
  transfers between devices with their start and end apart: 10 -> 10, of which waited for: 9 -> 9; matrix products, arithmetic and copies ran while one was open for 1% -> 2% of each run, Pallas kernels for 0% -> 0%
where the time goes in v1:
time: 130 us; the launch traced here: 129 us
  blocking collectives  45.3 us (35%)
  starting transfers between devices  30.9 us (24%)
  waiting for transfers between devices  20.1 us (15%)
  matrix products  12.1 us (9%)
  other arithmetic  11.2 us (9%)
  local copies, waits for them, and re-layouts  9.13 us (7%)
    all_to_all x1, blocking collectives, per_device(): lax.all_to_all(packed, 'exp', 0, 0, tiled=True)  25 us
    all_to_all x1, blocking collectives, per_device(): lax.all_to_all(jnp.stack([slot_out] * lax.axis_size('exp')), 'exp', 0, 0)  20.3 us
    ppermute x4, starting transfers between devices, butterfly_softmax_sum(): value = merge(value, lax.ppermute(value, axis, pairs))  13.4 us
    ppermute x4, starting transfers between devices, butterfly_sum(): value = value + lax.ppermute(value, axis, pairs)  11.1 us
    ppermute x4, waiting for transfers between devices, butterfly_sum(): value = value + lax.ppermute(value, axis, pairs)  9.47 us
    ppermute x4, waiting for transfers between devices, butterfly_softmax_sum(): value = merge(value, lax.ppermute(value, axis, pairs))  8.97 us
    reshape x1, local copies, waits for them, and re-layouts, per_device(): mixed.astype(jnp.bfloat16).reshape(periods, channels, D)  5.25 us
    another operation x7, other arithmetic  4.53 us
  transfers between devices with their start and end apart: 10, of which 9 were waited for; matrix products, arithmetic and copies ran while one was open for 2% of the time, Pallas kernels for 0%

profile of v1, /device:TPU:1, one launch (start us, length us, event | category | flops | bytes accessed | tf_op | source)
XLA Modules:
  0.0 129.0 jit_solution(14427451472551880548)
XLA Ops:
  1.3 4.5 %collective-permute-start = (bf16[4,1,256]{2,1,0:T(2,128)(2,1)S(1)}, bf16[4,1,256]{2,1,0:T(2,128)(2,1)S(1)}, u32[]{:S(2)}, u32[]{:S(2)}) collective-permute-start(bf16[4,1,256]{2,1,0:T(2,128)(2,1)S(1)} %get-tuple-element.116), channel_id=1, source_target_pairs={{0,1},{1,2},{2,3},{3,4},{4,5},{5,6},{6,7},{7,8},{8,9},{9,10},{10,1... | collective-permute-start | bytes 6152 | tf_op jit(solution)/shard_map/ppermute | solution.py:17
  5.8 1.9 %collective-permute-start.1 = (bf16[4,1,256]{2,1,0:T(2,128)(2,1)S(1)}, bf16[4,1,256]{2,1,0:T(2,128)(2,1)S(1)}, u32[]{:S(2)}, u32[]{:S(2)}) collective-permute-start(bf16[4,1,256]{2,1,0:T(2,128)(2,1)S(1)} %get-tuple-element.117), channel_id=1, source_target_pairs={{1,0},{2,1},{3,2},{4,3},{5,4},{6,5},{7,6},{8,7},{9,8},{10,9},{11,1... | collective-permute-start | bytes 6152 | tf_op jit(solution)/shard_map/ppermute | solution.py:18
  9.1 1.6 %collective-permute-done.1 = bf16[4,1,256]{2,1,0:T(2,128)(2,1)S(1)} collective-permute-done((bf16[4,1,256]{2,1,0:T(2,128)(2,1)S(1)}, bf16[4,1,256]{2,1,0:T(2,128)(2,1)S(1)}, u32[]{:S(2)}, u32[]{:S(2)}) %collective-permute-start.1) | collective-permute-done | bytes 2080 | tf_op jit(solution)/shard_map/ppermute | solution.py:18
  11.0 3.6 %convolution_convert_fusion.1 = bf16[1024,2048]{1,0:T(8,128)(2,1)S(1)} fusion(bf16[1024,768]{1,0:T(8,128)(2,1)S(1)} %bitcast.55, bf16[768,2048]{1,0:T(8,128)(2,1)S(1)} %bitcast.51), kind=kOutput, calls=%fused_computation.2 | convolution fusion | flops 3223322624 | bytes 8912896 | tf_op jit(solution)/shard_map/dot_general | solution.py:58
  16.0 1.7 %fusion.11 = f32[128,2048]{1,0:T(8,128)} fusion(bf16[1024,2048]{1,0:T(8,128)(2,1)S(1)} %convolution_convert_fusion.1, f32[1024,128]{1,0:T(8,128)S(1)} %get-tuple-element.118, f32[128]{0:T(128)S(1)} %get-tuple-element.104), kind=kOutput, calls=%fused_computation.22 | convolution fusion | flops 537133056 | bytes 5767680 | tf_op jit(solution)/shard_map/dot_general | solution.py:64
  21.3 25.0 %all_to_all.14 = f32[16,8,2176]{2,1,0:T(8,128)S(1)} all-to-all(f32[16,8,2176]{2,1,0:T(8,128)S(1)} %maximum_bitcast_fusion), channel_id=1, replica_groups=mesh['pos'=16,'exp'=16] {'exp'}, dimensions={0} | all-to-all | bytes 2228224 | tf_op jit(solution)/shard_map/all_to_all | solution.py:74
  51.0 1.7 %collective-permute-start.2 = (f32[8,2176]{1,0:T(8,128)S(1)}, f32[8,2176]{1,0:T(8,128)S(1)}, u32[]{:S(2)}, u32[]{:S(2)}) collective-permute-start(f32[8,2176]{1,0:T(8,128)S(1)} %pad_maximum_fusion.2), channel_id=1, source_target_pairs={{0,16},{16,0},{32,48},{48,32},{64,80},{80,64},{96,112},{112,96},{1... | collective-permute-start | bytes 208904 | tf_op jit(solution)/shard_map/ppermute | solution.py:46
  55.7 5.6 %collective-permute-start.3 = (f32[8,2176]{1,0:T(8,128)S(1)}, f32[8,2176]{1,0:T(8,128)S(1)}, u32[]{:S(2)}, u32[]{:S(2)}) collective-permute-start(f32[8,2176]{1,0:T(8,128)S(1)} %scatter.30), channel_id=1, source_target_pairs={{0,32},{16,48},{32,0},{48,16},{64,96},{80,112},{96,64},{112,80},{1... | collective-permute-start | bytes 208904 | tf_op jit(solution)/shard_map/ppermute | solution.py:46
  61.3 1.7 %collective-permute-done.3 = f32[8,2176]{1,0:T(8,128)S(1)} collective-permute-done((f32[8,2176]{1,0:T(8,128)S(1)}, f32[8,2176]{1,0:T(8,128)S(1)}, u32[]{:S(2)}, u32[]{:S(2)}) %collective-permute-start.3) | collective-permute-done | bytes 69664 | tf_op jit(solution)/shard_map/ppermute | solution.py:46
  64.0 3.2 %collective-permute-start.4 = (f32[8,2176]{1,0:T(8,128)S(1)}, f32[8,2176]{1,0:T(8,128)S(1)}, u32[]{:S(2)}, u32[]{:S(2)}) collective-permute-start(f32[8,2176]{1,0:T(8,128)S(1)} %scatter.31), channel_id=1, source_target_pairs={{0,64},{16,80},{32,96},{48,112},{64,0},{80,16},{96,32},{112,48},{1... | collective-permute-start | bytes 208904 | tf_op jit(solution)/shard_map/ppermute | solution.py:46
  67.2 4.0 %collective-permute-done.4 = f32[8,2176]{1,0:T(8,128)S(1)} collective-permute-done((f32[8,2176]{1,0:T(8,128)S(1)}, f32[8,2176]{1,0:T(8,128)S(1)}, u32[]{:S(2)}, u32[]{:S(2)}) %collective-permute-start.4) | collective-permute-done | bytes 69664 | tf_op jit(solution)/shard_map/ppermute | solution.py:46
  72.2 2.8 %collective-permute-start.5 = (f32[8,2176]{1,0:T(8,128)S(1)}, f32[8,2176]{1,0:T(8,128)S(1)}, u32[]{:S(2)}, u32[]{:S(2)}) collective-permute-start(f32[8,2176]{1,0:T(8,128)S(1)} %scatter.34), channel_id=1, source_target_pairs={{0,128},{16,144},{32,160},{48,176},{64,192},{80,208},{96,224},{112... | collective-permute-start | bytes 208904 | tf_op jit(solution)/shard_map/ppermute | solution.py:46
  75.0 1.9 %collective-permute-done.5 = f32[8,2176]{1,0:T(8,128)S(1)} collective-permute-done((f32[8,2176]{1,0:T(8,128)S(1)}, f32[8,2176]{1,0:T(8,128)S(1)}, u32[]{:S(2)}, u32[]{:S(2)}) %collective-permute-start.5) | collective-permute-done | bytes 69664 | tf_op jit(solution)/shard_map/ppermute | solution.py:46
  77.4 3.0 %fusion = f32[8,2048]{1,0:T(8,128)S(1)} fusion(bf16[1,512,2048]{2,1,0:T(8,128)(2,1)} %param.25, bf16[1,2048,512]{2,1,0:T(8,128)(2,1)} %param.24, f32[8,2176]{1,0:T(8,128)S(1)} %multiply_add_fusion, f32[8]{0:T(128)S(1)} %slice_reduce_fusion), kind=kOutput, calls=%fused_computation.3 | convolution fusion | flops 33624064 | bytes 4325888 | tf_op jit(solution)/shard_map/dot_general | solution.py:89
  81.7 1.8 %collective-permute-done.6 = f32[8,2048]{1,0:T(8,128)S(1)} collective-permute-done((f32[8,2048]{1,0:T(8,128)S(1)}, f32[8,2048]{1,0:T(8,128)S(1)}, u32[]{:S(2)}, u32[]{:S(2)}) %collective-permute-start.6) | collective-permute-done | bytes 65568 | tf_op jit(solution)/shard_map/ppermute | solution.py:28
  83.5 2.9 %collective-permute-start.7 = (f32[8,2048]{1,0:T(8,128)S(1)}, f32[8,2048]{1,0:T(8,128)S(1)}, u32[]{:S(2)}, u32[]{:S(2)}) collective-permute-start(f32[8,2048]{1,0:T(8,128)S(1)} %add.60), channel_id=1, source_target_pairs={{0,32},{16,48},{32,0},{48,16},{64,96},{80,112},{96,64},{112,80},{1... | collective-permute-start | bytes 196616 | tf_op jit(solution)/shard_map/ppermute | solution.py:28
  86.4 1.7 %collective-permute-done.7 = f32[8,2048]{1,0:T(8,128)S(1)} collective-permute-done((f32[8,2048]{1,0:T(8,128)S(1)}, f32[8,2048]{1,0:T(8,128)S(1)}, u32[]{:S(2)}, u32[]{:S(2)}) %collective-permute-start.7) | collective-permute-done | bytes 65568 | tf_op jit(solution)/shard_map/ppermute | solution.py:28
  88.1 3.2 %collective-permute-start.8 = (f32[8,2048]{1,0:T(8,128)S(1)}, f32[8,2048]{1,0:T(8,128)S(1)}, u32[]{:S(2)}, u32[]{:S(2)}) collective-permute-start(f32[8,2048]{1,0:T(8,128)S(1)} %add.61), channel_id=1, source_target_pairs={{0,64},{16,80},{32,96},{48,112},{64,0},{80,16},{96,32},{112,48},{1... | collective-permute-start | bytes 196616 | tf_op jit(solution)/shard_map/ppermute | solution.py:28
  91.3 4.3 %collective-permute-done.8 = f32[8,2048]{1,0:T(8,128)S(1)} collective-permute-done((f32[8,2048]{1,0:T(8,128)S(1)}, f32[8,2048]{1,0:T(8,128)S(1)}, u32[]{:S(2)}, u32[]{:S(2)}) %collective-permute-start.8) | collective-permute-done | bytes 65568 | tf_op jit(solution)/shard_map/ppermute | solution.py:28
  95.6 3.7 %collective-permute-start.9 = (f32[8,2048]{1,0:T(8,128)S(1)}, f32[8,2048]{1,0:T(8,128)S(1)}, u32[]{:S(2)}, u32[]{:S(2)}) collective-permute-start(f32[8,2048]{1,0:T(8,128)S(1)} %add.62), channel_id=1, source_target_pairs={{0,128},{16,144},{32,160},{48,176},{64,192},{80,208},{96,224},{112... | collective-permute-start | bytes 196616 | tf_op jit(solution)/shard_map/ppermute | solution.py:28
  99.4 1.7 %collective-permute-done.9 = f32[8,2048]{1,0:T(8,128)S(1)} collective-permute-done((f32[8,2048]{1,0:T(8,128)S(1)}, f32[8,2048]{1,0:T(8,128)S(1)}, u32[]{:S(2)}, u32[]{:S(2)}) %collective-permute-start.9) | collective-permute-done | bytes 65568 | tf_op jit(solution)/shard_map/ppermute | solution.py:28
  101.1 20.3 %all_to_all.15 = bf16[16,8,2048]{2,1,0:T(8,128)(2,1)S(1)} all-to-all(bf16[16,8,2048]{2,1,0:T(8,128)(2,1)S(1)} %stack.2), channel_id=1, replica_groups=mesh['pos'=16,'exp'=16] {'exp'}, dimensions={0} | all-to-all | bytes 1048576 | tf_op jit(solution)/shard_map/all_to_all | solution.py:97
  121.4 2.4 %convolution_convert_fusion = bf16[1024,2048]{1,0:T(8,128)(2,1)S(1)} fusion(bf16[16,8,2048]{2,1,0:T(8,128)(2,1)S(1)} %all_to_all.15, f32[1024,128]{1,0:T(8,128)} %copy-done.2, f32[1024]{0:T(1024)S(1)} %get-tuple-element.101, f32[1024]{0:T(1024)S(1)} %get-tuple-element.103), kind=kOutput, calls=%fused_computation.1 | convolution fusion | flops 539361280 | bytes 5251072 | tf_op jit(solution)/shard_map/dot_general | solution.py:94
  123.7 5.3 %copy.63 = bf16[4,256,2048]{2,0,1:T(4,128)(2,1)} copy(bf16[4,256,2048]{2,1,0:T(8,128)(2,1)S(1)} %bitcast.52) | data formatting | bytes 8388608 | tf_op jit(solution)/shard_map/reshape | solution.py:101
  (60 shorter events, 19.1 us)
Async XLA Ops:
  0.0 11.0 %copy-start = (bf16[3,256,2048]{2,1,0:T(8,128)(2,1)S(1)}, bf16[3,256,2048]{2,1,0:T(8,128)(2,1)}, u32[]{:S(2)}) copy-start(bf16[3,256,2048]{2,1,0:T(8,128)(2,1)} %param.22) | copy-start | bytes 9437188
  1.3 7.8 %collective-permute-start = (bf16[4,1,256]{2,1,0:T(2,128)(2,1)S(1)}, bf16[4,1,256]{2,1,0:T(2,128)(2,1)S(1)}, u32[]{:S(2)}, u32[]{:S(2)}) collective-permute-start(bf16[4,1,256]{2,1,0:T(2,128)(2,1)S(1)} %get-tuple-element.116), channel_id=1, source_target_pairs={{0,1},{1,2},{2,3},{3,4},{4,5},{5,6},{6,7},{7,8},{8,9},{9,10},{10,1... | collective-permute-start | bytes 6152 | tf_op jit(solution)/shard_map/ppermute | solution.py:17
  5.8 4.9 %collective-permute-start.1 = (bf16[4,1,256]{2,1,0:T(2,128)(2,1)S(1)}, bf16[4,1,256]{2,1,0:T(2,128)(2,1)S(1)}, u32[]{:S(2)}, u32[]{:S(2)}) collective-permute-start(bf16[4,1,256]{2,1,0:T(2,128)(2,1)S(1)} %get-tuple-element.117), channel_id=1, source_target_pairs={{1,0},{2,1},{3,2},{4,3},{5,4},{6,5},{7,6},{8,7},{9,8},{10,9},{11,1... | collective-permute-start | bytes 6152 | tf_op jit(solution)/shard_map/ppermute | solution.py:18
  11.0 3.7 %copy-start.3 = (bf16[2048,128]{1,0:T(8,128)(2,1)S(1)}, bf16[2048,128]{1,0:T(8,128)(2,1)}, u32[]{:S(2)}) copy-start(bf16[2048,128]{1,0:T(8,128)(2,1)} %param.23) | copy-start | bytes 1572868
  16.0 2.8 %copy-start.2 = (f32[1024,128]{1,0:T(8,128)}, f32[1024,128]{1,0:T(8,128)S(1)}, u32[]{:S(2)}) copy-start(f32[1024,128]{1,0:T(8,128)S(1)} %get-tuple-element.118) | copy-start | bytes 1572868
  46.4 1.0 copy-start.1
  51.0 3.7 %collective-permute-start.2 = (f32[8,2176]{1,0:T(8,128)S(1)}, f32[8,2176]{1,0:T(8,128)S(1)}, u32[]{:S(2)}, u32[]{:S(2)}) collective-permute-start(f32[8,2176]{1,0:T(8,128)S(1)} %pad_maximum_fusion.2), channel_id=1, source_target_pairs={{0,16},{16,0},{32,48},{48,32},{64,80},{80,64},{96,112},{112,96},{1... | collective-permute-start | bytes 208904 | tf_op jit(solution)/shard_map/ppermute | solution.py:46
  55.7 7.3 %collective-permute-start.3 = (f32[8,2176]{1,0:T(8,128)S(1)}, f32[8,2176]{1,0:T(8,128)S(1)}, u32[]{:S(2)}, u32[]{:S(2)}) collective-permute-start(f32[8,2176]{1,0:T(8,128)S(1)} %scatter.30), channel_id=1, source_target_pairs={{0,32},{16,48},{32,0},{48,16},{64,96},{80,112},{96,64},{112,80},{1... | collective-permute-start | bytes 208904 | tf_op jit(solution)/shard_map/ppermute | solution.py:46
  64.0 7.2 %collective-permute-start.4 = (f32[8,2176]{1,0:T(8,128)S(1)}, f32[8,2176]{1,0:T(8,128)S(1)}, u32[]{:S(2)}, u32[]{:S(2)}) collective-permute-start(f32[8,2176]{1,0:T(8,128)S(1)} %scatter.31), channel_id=1, source_target_pairs={{0,64},{16,80},{32,96},{48,112},{64,0},{80,16},{96,32},{112,48},{1... | collective-permute-start | bytes 208904 | tf_op jit(solution)/shard_map/ppermute | solution.py:46
  72.2 4.8 %collective-permute-start.5 = (f32[8,2176]{1,0:T(8,128)S(1)}, f32[8,2176]{1,0:T(8,128)S(1)}, u32[]{:S(2)}, u32[]{:S(2)}) collective-permute-start(f32[8,2176]{1,0:T(8,128)S(1)} %scatter.34), channel_id=1, source_target_pairs={{0,128},{16,144},{32,160},{48,176},{64,192},{80,208},{96,224},{112... | collective-permute-start | bytes 208904 | tf_op jit(solution)/shard_map/ppermute | solution.py:46
  80.4 3.1 %collective-permute-start.6 = (f32[8,2048]{1,0:T(8,128)S(1)}, f32[8,2048]{1,0:T(8,128)S(1)}, u32[]{:S(2)}, u32[]{:S(2)}) collective-permute-start(f32[8,2048]{1,0:T(8,128)S(1)} %fusion), channel_id=1, source_target_pairs={{0,16},{16,0},{32,48},{48,32},{64,80},{80,64},{96,112},{112,96},{1... | collective-permute-start | bytes 196616 | tf_op jit(solution)/shard_map/ppermute | solution.py:28
  83.5 4.6 %collective-permute-start.7 = (f32[8,2048]{1,0:T(8,128)S(1)}, f32[8,2048]{1,0:T(8,128)S(1)}, u32[]{:S(2)}, u32[]{:S(2)}) collective-permute-start(f32[8,2048]{1,0:T(8,128)S(1)} %add.60), channel_id=1, source_target_pairs={{0,32},{16,48},{32,0},{48,16},{64,96},{80,112},{96,64},{112,80},{1... | collective-permute-start | bytes 196616 | tf_op jit(solution)/shard_map/ppermute | solution.py:28
  88.1 7.5 %collective-permute-start.8 = (f32[8,2048]{1,0:T(8,128)S(1)}, f32[8,2048]{1,0:T(8,128)S(1)}, u32[]{:S(2)}, u32[]{:S(2)}) collective-permute-start(f32[8,2048]{1,0:T(8,128)S(1)} %add.61), channel_id=1, source_target_pairs={{0,64},{16,80},{32,96},{48,112},{64,0},{80,16},{96,32},{112,48},{1... | collective-permute-start | bytes 196616 | tf_op jit(solution)/shard_map/ppermute | solution.py:28
  95.6 5.4 %collective-permute-start.9 = (f32[8,2048]{1,0:T(8,128)S(1)}, f32[8,2048]{1,0:T(8,128)S(1)}, u32[]{:S(2)}, u32[]{:S(2)}) collective-permute-start(f32[8,2048]{1,0:T(8,128)S(1)} %add.62), channel_id=1, source_target_pairs={{0,128},{16,144},{32,160},{48,176},{64,192},{80,208},{96,224},{112... | collective-permute-start | bytes 196616 | tf_op jit(solution)/shard_map/ppermute | solution.py:28
